TPU v7x, 32 devices: a whole 2x2x4 slice. The times are simulated.
32 devices in a mesh: cp: 2 (over y), tp: 4 (over x, core), ep: 4 (over z).
Axes of the slice: x: 2, y: 2, z: 4, core: 2. Of those that a mesh axis runs over, the one named last changes fastest.
Arguments:
- query: bfloat16 [8, 512, 4096], P('ep', 'cp', 'tp'), may hold values from -6 to 6
- keys: bfloat16 [8, 512, 512], P('ep', 'cp', 'tp'), may hold values from -6 to 6
- values: bfloat16 [8, 512, 512], P('ep', 'cp', 'tp'), may hold values from -24 to 24
- segment_ids: int32 [8, 512], P('ep', 'cp'), may hold values from 0 to 3, never falling along the last dimension, each value on 1 to 256 neighbouring positions
- query_norm_gain: float32 [128], replicated, may hold values from 0.25 to 1.75
- key_norm_gain: float32 [128], replicated, may hold values from 0.25 to 1.75
- out_weight: bfloat16 [4096, 2048], P('tp', 'cp'), may hold values from -0.09375 to 0.09375
- residual: bfloat16 [8, 512, 2048], P('ep', 'cp'), may hold values from -3 to 3
- norm_gain: float32 [2048], replicated, may hold values from 0.25 to 1.75
- router_weight: bfloat16 [2048, 16], replicated, may hold values from -0.125 to 0.125
- expert_ids: int32 [8, 512, 8], P('ep', 'cp'), may hold values from 0 to 15, all different within a row; in each aligned block of 64 rows (0 to 63, 64 to 127, ..., all dimensions but the last counted through in order) at most 36 rows name the same one
- expert_gate: bfloat16 [16, 2048, 768], P(('tp', 'ep'), None, 'cp'), may hold values from -0.125 to 0.125
- expert_up: bfloat16 [16, 2048, 768], P(('tp', 'ep'), None, 'cp'), may hold values from -0.125 to 0.125
- expert_down: bfloat16 [16, 2048, 768], P(('tp', 'ep'), None, 'cp'), may hold values from -0.21875 to 0.21875
Outputs:
- layer_out: bfloat16 [8, 512, 2048], P('ep', ('cp', 'tp'))
Inputs may be any that keep to these rules, and one draw needn't show every extreme that they name: `segment_ids`: document numbers never fall along a sequence. `expert_ids`: each token names 8 different experts; in every aligned block of 64 positions of a sequence no expert is named by more than 36 tokens, a bound that some block reaches.
All inputs are finite; a program needn't handle non-finite values.
Results may differ from a plain program's by a relative error of at most 0.007.
Values may be sent and summed in bfloat16 or wider, within the bound.
No kernel may reach another device: no remote copies, remote signals or barrier semaphores. Data moves between devices by JAX's collectives and lax.ppermute only.
A program may use at most 128 MiB of HBM per device.

v0:
```python
import functools
import jax
import jax.numpy as jnp
from jax import lax
from jax.sharding import PartitionSpec as P

HEAD_WIDTH = 128


def root_mean_scale(entries, gain):
    mean_sq = jnp.mean(entries * entries, axis=-1, keepdims=True)
    return entries * lax.rsqrt(mean_sq + 1e-06) * gain


def capacity(share, top_count, experts):
    return min(
        share, max(2, share * top_count // experts + max(1, share * top_count // (8 * experts)))
    )


def slot_numbers(ids, experts):
    flat_ids = ids.reshape(-1)
    table = (flat_ids[:, None] == jnp.arange(experts, dtype=jnp.int32)[None, :]).astype(jnp.int32)
    before = jnp.cumsum(table, axis=0) - table
    return jnp.sum(before * table, axis=1).reshape(ids.shape)


def route(state, ids, norm_gain, router_weight):
    normed = root_mean_scale(state, norm_gain).astype(jnp.bfloat16)
    logits = jnp.dot(normed, router_weight, preferred_element_type=jnp.float32)
    experts = router_weight.shape[1]
    picks = ids[:, :, None] == jnp.arange(experts, dtype=jnp.int32)[None, None, :]
    chosen = jnp.sum(jnp.where(picks, logits[:, None, :], jnp.float32(0.0)), axis=-1)
    raised = jnp.exp(chosen)
    return (normed, raised / jnp.sum(raised, axis=-1, keepdims=True))


def cp_pieces(x, n_cp):
    pieces = [x]
    for shift in range(1, n_cp):
        perm = [(i, (i + shift) % n_cp) for i in range(n_cp)]
        pieces.append(lax.ppermute(x, "cp", perm))
    return pieces


def expert_rows(received, full_gate, full_up, full_down):
    width = received.shape[-1]
    flat_rows = received.reshape(-1, width)
    gate_act = jnp.dot(flat_rows, full_gate[0], preferred_element_type=jnp.float32)
    up_act = jnp.dot(flat_rows, full_up[0], preferred_element_type=jnp.float32)
    hidden_act = (jax.nn.silu(gate_act) * up_act).astype(jnp.bfloat16)
    served = jnp.einsum(
        "rf,df->rd", hidden_act, full_down[0], preferred_element_type=jnp.float32
    ).astype(jnp.bfloat16)
    return served.reshape(received.shape)


def shards(
    query,
    keys,
    values,
    segment_ids,
    query_norm_gain,
    key_norm_gain,
    out_weight,
    residual,
    norm_gain,
    router_weight,
    expert_ids,
    expert_gate,
    expert_up,
    expert_down,
    *,
    n_cp,
    n_tp,
    n_ep
):
    packs = query.shape[0]
    row_count = query.shape[1]
    head_count = query.shape[2] // HEAD_WIDTH
    width = residual.shape[2]
    experts = router_weight.shape[1]
    top_count = expert_ids.shape[2]
    score_scale = HEAD_WIDTH ** (-0.5)
    query_rows_normed = root_mean_scale(
        query.astype(jnp.float32).reshape(packs, row_count, head_count, HEAD_WIDTH), query_norm_gain
    ).astype(jnp.bfloat16)
    key_rows_normed = root_mean_scale(keys.astype(jnp.float32), key_norm_gain).astype(jnp.bfloat16)
    key_value = jnp.concatenate([key_rows_normed, values], axis=-1)
    kv_all = jnp.concatenate(cp_pieces(key_value, n_cp), axis=1)
    doc_all = jnp.concatenate(cp_pieces(segment_ids, n_cp), axis=1)
    key_piece = kv_all[..., :HEAD_WIDTH]
    value_piece = kv_all[..., HEAD_WIDTH:]
    scores = (
        jnp.einsum(
            "pshd,pnd->phsn", query_rows_normed, key_piece, preferred_element_type=jnp.float32
        )
        * score_scale
    )
    same_doc = segment_ids[:, :, None] == doc_all[:, None, :]
    probs = jnp.where(same_doc[:, None], jnp.exp(scores), jnp.float32(0.0))
    denom = jnp.sum(probs, axis=-1)
    probs_b = probs.astype(jnp.bfloat16)
    summed = jnp.einsum("phsn,pnd->pshd", probs_b, value_piece, preferred_element_type=jnp.float32)
    attn = (
        (summed / jnp.transpose(denom, (0, 2, 1))[:, :, :, None])
        .astype(jnp.bfloat16)
        .reshape(packs * row_count, head_count * HEAD_WIDTH)
    )
    share = row_count // n_tp
    tp_index = lax.axis_index("tp")
    ep_index = lax.axis_index("ep")
    cp_index = lax.axis_index("cp")
    cap = capacity(share, top_count, experts)
    attn_pieces = cp_pieces(attn, n_cp)
    received_blocks = []
    for j, piece in enumerate(attn_pieces):
        if j > 0:
            piece, received_blocks[0] = lax.optimization_barrier((piece, received_blocks[0]))
        block = jnp.dot(piece, out_weight, preferred_element_type=jnp.float32).reshape(
            packs, row_count, out_weight.shape[1]
        )
        summed = lax.psum_scatter(block.astype(jnp.bfloat16), "tp", scatter_dimension=1, tiled=True)
        if j > 0:
            summed = lax.ppermute(summed, "cp", [(i, (i - j) % n_cp) for i in range(n_cp)])
        received_blocks.append(summed)
    blocks = jnp.stack(received_blocks, axis=2).astype(jnp.float32)
    source_block = (jnp.arange(n_cp, dtype=jnp.int32) - cp_index) % n_cp
    picks_block = source_block[:, None] == jnp.arange(n_cp, dtype=jnp.int32)[None, :]
    projected = jnp.sum(
        jnp.where(picks_block[None, None, :, :, None], blocks[:, :, None, :, :], jnp.float32(0.0)),
        axis=3,
    ).reshape(packs, share, width)
    first_row = tp_index * share
    state = lax.dynamic_slice_in_dim(residual, first_row, share, 1).astype(jnp.float32) + projected
    local_ids = lax.dynamic_slice_in_dim(expert_ids, first_row, share, 1).reshape(
        packs * share, top_count
    )
    home_rows = packs * share
    normed = root_mean_scale(state.reshape(home_rows, width), norm_gain).astype(jnp.bfloat16)
    attn_pieces, expert_gate, expert_up, expert_down = lax.optimization_barrier(
        (attn_pieces, expert_gate, expert_up, expert_down)
    )
    gate_pieces = cp_pieces(expert_gate, n_cp)
    normed, gate_pieces = lax.optimization_barrier((normed, gate_pieces))
    up_down = jnp.concatenate([expert_up, expert_down], axis=2)
    gate_pieces, up_down = lax.optimization_barrier((gate_pieces, up_down))
    up_down_pieces = cp_pieces(up_down, n_cp)
    lanes = 128
    cap2 = n_ep * cap
    n_slots = n_tp * cap2
    gathered = n_ep * share
    row_iota = jnp.arange(gathered, dtype=jnp.int32)
    earlier = (row_iota[:, None] > row_iota[None, :]).astype(jnp.bfloat16)
    contract = (((0,), (0,)), ((), ()))
    id_lanes = jnp.pad(local_ids.astype(jnp.bfloat16), ((0, 0), (0, lanes - top_count)))
    rows_with_ids = jnp.concatenate([normed, id_lanes], axis=1)
    mixtures = []
    for chunk in range(packs):
        rows = rows_with_ids[chunk * share : (chunk + 1) * share]
        if chunk > 0:
            rows, _ = lax.optimization_barrier((rows, buffer))
        rows_all = lax.all_gather(rows, "ep", axis=0, tiled=True)
        normed_all = rows_all[:, :width]
        ids_all = rows_all[:, width : width + top_count].astype(jnp.int32)
        logits = jnp.dot(normed_all, router_weight, preferred_element_type=jnp.float32)
        picks = ids_all[:, :, None] == jnp.arange(experts, dtype=jnp.int32)[None, None, :]
        raised = jnp.exp(jnp.sum(jnp.where(picks, logits[:, None, :], jnp.float32(0.0)), axis=-1))
        gates_all = raised / jnp.sum(raised, axis=-1, keepdims=True)
        mine = ids_all % n_ep == ep_index
        dest = ids_all // n_ep
        named = jnp.stack(
            [jnp.any(mine & (dest == j), axis=1) for j in range(n_tp)], axis=1
        ).astype(jnp.bfloat16)
        rank = jnp.dot(earlier, named, preferred_element_type=jnp.float32).astype(jnp.int32)
        rank_of = jnp.sum(
            jnp.where(
                dest[:, :, None] == jnp.arange(n_tp, dtype=jnp.int32)[None, None, :],
                rank[:, None, :],
                0,
            ),
            axis=-1,
        )
        target = jnp.where(mine, dest * cap2 + rank_of, jnp.int32(-1)).T
        if chunk == 0:
            full_gate = jnp.concatenate(gate_pieces, axis=2)
        hit = target[:, None, :] == jnp.arange(n_slots, dtype=jnp.int32)[None, :, None]
        select = jnp.any(hit, axis=0).astype(jnp.bfloat16)
        weight = jnp.sum(jnp.where(hit, gates_all.T[:, None, :], jnp.float32(0.0)), axis=0)
        buffer = jnp.dot(select, normed_all, preferred_element_type=jnp.float32).astype(
            jnp.bfloat16
        )
        received = lax.all_to_all(
            buffer.reshape(n_tp, cap2, width), "tp", split_axis=0, concat_axis=0, tiled=True
        )
        if chunk == 0:
            received, up_down_pieces = lax.optimization_barrier((received, up_down_pieces))
            units = expert_up.shape[2]
            full_up = jnp.concatenate([p[:, :, :units] for p in up_down_pieces], axis=2)
            full_down = jnp.concatenate([p[:, :, units:] for p in up_down_pieces], axis=2)
        served = expert_rows(received, full_gate, full_up, full_down)
        back = lax.all_to_all(served, "tp", split_axis=0, concat_axis=0, tiled=True).reshape(
            n_slots, width
        )
        weight_hi = weight.astype(jnp.bfloat16)
        weight_lo = (weight - weight_hi.astype(jnp.float32)).astype(jnp.bfloat16)
        partial = lax.dot_general(
            weight_hi, back, contract, preferred_element_type=jnp.float32
        ) + lax.dot_general(weight_lo, back, contract, preferred_element_type=jnp.float32)
        mixtures.append(
            lax.psum_scatter(
                partial.astype(jnp.bfloat16).reshape(n_ep, share, width),
                "ep",
                scatter_dimension=0,
                tiled=True,
            )
        )
    mixture = jnp.concatenate(mixtures, axis=0).astype(jnp.float32)
    layer_out = (state + mixture).astype(jnp.bfloat16)
    return layer_out


def solution(mesh):
    body = functools.partial(
        shards, n_cp=mesh.shape["cp"], n_tp=mesh.shape["tp"], n_ep=mesh.shape["ep"]
    )
    return jax.shard_map(
        body,
        mesh=mesh,
        in_specs=(
            P("ep", "cp", "tp"),
            P("ep", "cp", "tp"),
            P("ep", "cp", "tp"),
            P("ep", "cp"),
            P(),
            P(),
            P("tp", "cp"),
            P("ep", "cp", None),
            P(),
            P(),
            P("ep", "cp", None),
            P(("tp", "ep"), None, "cp"),
            P(("tp", "ep"), None, "cp"),
            P(("tp", "ep"), None, "cp"),
        ),
        out_specs=P("ep", ("cp", "tp"), None),
        check_vma=False,
    )
```

profile of v0, /device:TPU:0, one launch (start us, length us, event | category | flops | bytes accessed | tf_op | source)
XLA Modules:
  0.0 310.7 jit_solution(364503522960644901)
XLA Ops:
  6.5 3.0 collective-permute-start.1
  30.1 23.3 %collective-permute-done.2 = bf16[512,1024]{1,0:T(8,128)(2,1)S(1)} collective-permute-done((bf16[512,1024]{1,0:T(8,128)(2,1)S(1)}, bf16[512,1024]{1,0:T(8,128)(2,1)S(1)}, u32[]{:S(2)}, u32[]{:S(2)}) %collective-permute-start.2) | collective-permute-done | bytes 1048608 | tf_op jit(solution)/shard_map/ppermute | solution.py:42
  56.9 24.5 %reduce-scatter.7.cloned.1.call-done = bf16[2,64,1024]{2,1,0:T(8,128)(2,1)} async-done(((bf16[2,256,1024]{2,1,0:T(8,128)(2,1)}), bf16[2,64,1024]{2,1,0:T(8,128)(2,1)}) %reduce-scatter.7.cloned.1.call-update) | async-done | bytes 262160 | tf_op jit(solution)/shard_map/reduce_scatter | solution.py:123
  83.0 14.3 %collective-permute-done.3 = bf16[2,64,1024]{2,1,0:T(8,128)(2,1)S(1)} collective-permute-done((bf16[2,64,1024]{2,1,0:T(8,128)(2,1)}, bf16[2,64,1024]{2,1,0:T(8,128)(2,1)S(1)}, u32[]{:S(2)}, u32[]{:S(2)}) %collective-permute-start.3) | collective-permute-done | bytes 262176 | tf_op jit(solution)/shard_map/ppermute | solution.py:125
  100.3 3.8 %pad_maximum_fusion = bf16[1,2048,768]{2,1,0:T(8,128)(2,1)} fusion(bf16[1,2048,384]{2,1,0:T(8,128)(2,1)} %param.27, bf16[1,2048,384]{2,1,0:T(8,128)(2,1)} %param.26), kind=kLoop, calls=%fused_computation.13 | loop fusion | flops 6291456 | bytes 6291456 | tf_op jit(solution)/shard_map/concatenate | solution.py:146
  105.6 23.9 %all-gather.3.cloned.1.call-done = bf16[256,2176]{1,0:T(8,128)(2,1)} async-done(((bf16[64,2176]{1,0:T(8,128)(2,1)}), bf16[256,2176]{1,0:T(8,128)(2,1)}) %all-gather.3.cloned.1.call-update) | async-done | bytes 1114128 | tf_op jit(solution)/shard_map/all_gather | solution.py:163
  131.5 3.4 %convolution_convert_fusion.3 = bf16[576,2048]{1,0:T(8,128)(2,1)} fusion(pred[576,256]{1,0:T(8,128)(4,1)S(1)} %fusion.3, bf16[256,2176]{1,0:T(8,128)(2,1)} %all-gather.3.cloned.1.call-done), kind=kOutput, calls=%fused_computation.20 | convolution fusion | flops 605159424 | bytes 3555328 | tf_op jit(solution)/shard_map/dot_general | solution.py:190
  135.0 4.8 %all-to-all-start = ((bf16[4,144,2048]{2,1,0:T(8,128)(2,1)}), bf16[4,144,2048]{2,1,0:T(8,128)(2,1)}, u32[]{:S(2)}, u32[]{:S(2)}) async-start(bf16[4,144,2048]{2,1,0:T(8,128)(2,1)} %bitcast.119), calls=%async_computation.2 | async-start | bytes 4718592 | tf_op jit(solution)/shard_map/all_to_all | solution.py:193
  140.3 23.3 %all-gather.5.cloned.1.call-done = bf16[256,2176]{1,0:T(8,128)(2,1)} async-done(((bf16[64,2176]{1,0:T(8,128)(2,1)}), bf16[256,2176]{1,0:T(8,128)(2,1)}) %all-gather.5.cloned.1.call-update) | async-done | bytes 1114128 | tf_op jit(solution)/shard_map/all_gather | solution.py:163
  165.6 3.4 %convolution_convert_fusion.2 = bf16[576,2048]{1,0:T(8,128)(2,1)} fusion(pred[576,256]{1,0:T(8,128)(4,1)S(1)} %fusion.2, bf16[256,2176]{1,0:T(8,128)(2,1)} %all-gather.5.cloned.1.call-done), kind=kOutput, calls=%fused_computation.19 | convolution fusion | flops 605159424 | bytes 3555328 | tf_op jit(solution)/shard_map/dot_general | solution.py:190
  169.0 4.6 %all-to-all-start.2 = ((bf16[4,144,2048]{2,1,0:T(8,128)(2,1)}), bf16[4,144,2048]{2,1,0:T(8,128)(2,1)}, u32[]{:S(2)}, u32[]{:S(2)}) async-start(bf16[4,144,2048]{2,1,0:T(8,128)(2,1)} %bitcast.120), calls=%async_computation.5 | async-start | bytes 4718592 | tf_op jit(solution)/shard_map/all_to_all | solution.py:193
  173.7 5.4 %fusion.20 = f32[576,768]{1,0:T(8,128)} fusion(bf16[576,2048]{1,0:T(8,128)(2,1)} %bitcast.16, bf16[1,2048,384]{2,1,0:T(8,128)(2,1)} %collective-permute-done.4, bf16[1,2048,384]{2,1,0:T(8,128)(2,1)S(1)} %copy-done.13), kind=kOutput, calls=%fused_computation.38 | convolution fusion | flops 1818230784 | bytes 7274496 | tf_op jit(solution)/shard_map/dot_general | solution.py:49
  179.1 5.2 %fusion.82 = (bf16[1,2048,384]{2,1,0:T(8,128)(2,1)S(1)}, bf16[1,2048,384]{2,1,0:T(8,128)(2,1)}, bf16[1,2048,384]{2,1,0:T(8,128)(2,1)}, bf16[1,2048,384]{2,1,0:T(8,128)(2,1)}) fusion(bf16[1,2048,768]{2,1,0:T(8,128)(2,1)} %pad_maximum_fusion, bf16[1,2048,768]{2,1,0:T(8,128)(2,1)} %collective-permute-done.5), kind=kLoop, calls=%fused_computation.157 | loop fusion | bytes 12582912 | tf_op jit(solution)/shard_map/slice | solution.py:199
  184.3 9.4 %convolution_convert_fusion.1 = bf16[576,2048]{1,0:T(8,128)(2,1)} fusion(bf16[1,2048,384]{2,1,0:T(8,128)(2,1)} %get-tuple-element.57, bf16[1,2048,384]{2,1,0:T(8,128)(2,1)} %get-tuple-element.50, f32[576,768]{1,0:T(8,128)} %fusion.20, bf16[576,2048]{1,0:T(8,128)(2,1)} %bitcast.16, bf16[1,2048,384]{2,1,0:T(8,128)(2,1)} %get-tuple-element.58, ...), kind=kOutput, calls=%fused_computation.18 | convolution fusion | flops 3640295424 | bytes 12779520 | tf_op jit(solution)/shard_map/rf,df->rd/dot_general | solution.py:52
  193.6 8.6 %all-to-all-done.2 = bf16[4,144,2048]{2,1,0:T(8,128)(2,1)} async-done(((bf16[4,144,2048]{2,1,0:T(8,128)(2,1)}), bf16[4,144,2048]{2,1,0:T(8,128)(2,1)}, u32[]{:S(2)}, u32[]{:S(2)}) %all-to-all-start.2) | async-done | bytes 2359328 | tf_op jit(solution)/shard_map/all_to_all | solution.py:193
  202.2 4.7 %all-to-all-start.1 = ((bf16[4,144,2048]{2,1,0:T(8,128)(2,1)}), bf16[4,144,2048]{2,1,0:T(8,128)(2,1)}, u32[]{:S(2)}, u32[]{:S(2)}) async-start(bf16[4,144,2048]{2,1,0:T(8,128)(2,1)} %bitcast.128), calls=%async_computation.3 | async-start | bytes 4718592 | tf_op jit(solution)/shard_map/all_to_all | solution.py:202
  208.4 5.8 %fusion.19 = f32[576,768]{1,0:T(8,128)} fusion(bf16[576,2048]{1,0:T(8,128)(2,1)} %bitcast.26, bf16[1,2048,384]{2,1,0:T(8,128)(2,1)} %collective-permute-done.4, bf16[1,2048,384]{2,1,0:T(8,128)(2,1)} %param.25), kind=kOutput, calls=%fused_computation.37 | convolution fusion | flops 1818230784 | bytes 7274496 | tf_op jit(solution)/shard_map/dot_general | solution.py:49
  214.2 9.4 %convolution_convert_fusion = bf16[576,2048]{1,0:T(8,128)(2,1)} fusion(bf16[1,2048,384]{2,1,0:T(8,128)(2,1)} %get-tuple-element.57, bf16[1,2048,384]{2,1,0:T(8,128)(2,1)} %get-tuple-element.50, f32[576,768]{1,0:T(8,128)} %fusion.19, bf16[576,2048]{1,0:T(8,128)(2,1)} %bitcast.26, bf16[1,2048,384]{2,1,0:T(8,128)(2,1)} %get-tuple-element.58, ...), kind=kOutput, calls=%fused_computation.17 | convolution fusion | flops 3640295424 | bytes 12779520 | tf_op jit(solution)/shard_map/rf,df->rd/dot_general | solution.py:52
  223.7 11.6 %all-to-all-done.1 = bf16[4,144,2048]{2,1,0:T(8,128)(2,1)} async-done(((bf16[4,144,2048]{2,1,0:T(8,128)(2,1)}), bf16[4,144,2048]{2,1,0:T(8,128)(2,1)}, u32[]{:S(2)}, u32[]{:S(2)}) %all-to-all-start.1) | async-done | bytes 2359328 | tf_op jit(solution)/shard_map/all_to_all | solution.py:202
  235.3 4.5 %all-to-all-start.3 = ((bf16[4,144,2048]{2,1,0:T(8,128)(2,1)}), bf16[4,144,2048]{2,1,0:T(8,128)(2,1)}, u32[]{:S(2)}, u32[]{:S(2)}) async-start(bf16[4,144,2048]{2,1,0:T(8,128)(2,1)} %bitcast.127), calls=%async_computation.6 | async-start | bytes 4718592 | tf_op jit(solution)/shard_map/all_to_all | solution.py:202
  242.8 3.7 %fusion.9 = bf16[256,2048]{1,0:T(8,128)(2,1)} fusion(f32[256,2048]{1,0:T(8,128)S(1)} %fusion.45, bf16[576,2048]{1,0:T(8,128)(2,1)} %bitcast.21, f32[576,256]{1,0:T(8,128)S(1)} %copy-done.3), kind=kOutput, calls=%fused_computation.23 | convolution fusion | flops 605618176 | bytes 6094848 | tf_op jit(solution)/shard_map/dot_general | solution.py:209
  248.9 19.5 %all-to-all-done.3 = bf16[4,144,2048]{2,1,0:T(8,128)(2,1)} async-done(((bf16[4,144,2048]{2,1,0:T(8,128)(2,1)}), bf16[4,144,2048]{2,1,0:T(8,128)(2,1)}, u32[]{:S(2)}, u32[]{:S(2)}) %all-to-all-start.3) | async-done | bytes 2359328 | tf_op jit(solution)/shard_map/all_to_all | solution.py:202
  271.1 4.2 %fusion.10 = bf16[256,2048]{1,0:T(8,128)(2,1)} fusion(f32[256,2048]{1,0:T(8,128)S(1)} %fusion.42, bf16[576,2048]{1,0:T(8,128)(2,1)} %bitcast.28, f32[576,256]{1,0:T(8,128)} %copy-done.4), kind=kOutput, calls=%fused_computation.24 | convolution fusion | flops 605618176 | bytes 6094848 | tf_op jit(solution)/shard_map/dot_general | solution.py:209
  275.4 26.5 %reduce-scatter.11.cloned.1.call-done = bf16[1,64,2048]{2,1,0:T(8,128)(2,1)} async-done(((bf16[4,64,2048]{2,1,0:T(8,128)(2,1)}), bf16[1,64,2048]{2,1,0:T(8,128)(2,1)}) %reduce-scatter.11.cloned.1.call-update) | async-done | bytes 262160 | tf_op jit(solution)/shard_map/reduce_scatter | solution.py:211
  (122 shorter events, 45.8 us)
Async XLA Ops:
  6.5 18.7 %copy-start = (bf16[1024,1024]{1,0:T(8,128)(2,1)S(1)}, bf16[1024,1024]{1,0:T(8,128)(2,1)}, u32[]{:S(2)}) copy-start(bf16[1024,1024]{1,0:T(8,128)(2,1)} %param.20) | copy-start | bytes 6291460
  6.5 46.8 %reduce-scatter.5.cloned.1.call-start = ((), (), s32[]{:S(2)}) async-start(), calls=%async_computation.8 | async-start | bytes 1310720 | tf_op jit(solution)/shard_map/reduce_scatter | solution.py:123
  6.5 12.0 %collective-permute-start.1 = (s32[2,256]{1,0:T(2,128)}, s32[2,256]{1,0:T(2,128)S(1)}, u32[]{:S(2)}, u32[]{:S(2)}) collective-permute-start(s32[2,256]{1,0:T(2,128)} %param.17), channel_id=1, source_target_pairs={{0,16},{16,0},{1,17},{17,1},{2,18},{18,2},{3,19},{19,3},{4,20},{20... | collective-permute-start | bytes 6152 | tf_op jit(solution)/shard_map/ppermute | solution.py:42
  12.6 7.8 %collective-permute-start = (bf16[2,256,256]{2,1,0:T(8,128)(2,1)S(1)}, bf16[2,256,256]{2,1,0:T(8,128)(2,1)S(1)}, u32[]{:S(2)}, u32[]{:S(2)}) collective-permute-start(bf16[2,256,256]{2,1,0:T(8,128)(2,1)S(1)} %pad_maximum_fusion.2), channel_id=1, source_target_pairs={{0,16},{16,0},{1,17},{17,1},{2,18},{18,2},{3,19},{19,3},{4,20},{20... | collective-permute-start | bytes 786440 | tf_op jit(solution)/shard_map/ppermute | solution.py:42
  27.5 53.8 %reduce-scatter.7.cloned.1.call-start = ((), (), s32[]{:S(2)}) async-start(), calls=%async_computation.9 | async-start | bytes 1310720 | tf_op jit(solution)/shard_map/reduce_scatter | solution.py:123
  29.6 27.2 %copy-start.11 = (s32[2,256,8]{1,2,0:T(8,128)S(1)}, s32[2,256,8]{1,2,0:T(8,128)}, u32[]{:S(2)}) copy-start(s32[2,256,8]{1,2,0:T(8,128)} %param.24) | copy-start | bytes 49156
  29.6 23.8 %collective-permute-start.2 = (bf16[512,1024]{1,0:T(8,128)(2,1)S(1)}, bf16[512,1024]{1,0:T(8,128)(2,1)S(1)}, u32[]{:S(2)}, u32[]{:S(2)}) collective-permute-start(bf16[512,1024]{1,0:T(8,128)(2,1)S(1)} %bitcast.131), channel_id=1, source_target_pairs={{0,16},{16,0},{1,17},{17,1},{2,18},{18,2},{3,19},{19,3},{4,20},{20... | collective-permute-start | bytes 3145736 | tf_op jit(solution)/shard_map/ppermute | solution.py:42
  53.4 43.9 %copy-start.8 = (bf16[2,64,1024]{2,1,0:T(8,128)(2,1)S(1)}, bf16[2,64,1024]{2,1,0:T(8,128)(2,1)}, u32[]{:S(2)}) copy-start(bf16[2,64,1024]{2,1,0:T(8,128)(2,1)} %reduce-scatter.5.cloned.1.call-done) | copy-start | bytes 786436
  55.7 73.8 %all-gather.3.cloned.1.call-start = ((), (), s32[]{:S(2)}) async-start(), calls=%async_computation.10 | async-start | bytes 1392640 | tf_op jit(solution)/shard_map/all_gather | solution.py:163
  55.7 43.6 %collective-permute-start.4 = (bf16[1,2048,384]{2,1,0:T(8,128)(2,1)}, bf16[1,2048,384]{2,1,0:T(8,128)(2,1)}, u32[]{:S(2)}, u32[]{:S(2)}) collective-permute-start(bf16[1,2048,384]{2,1,0:T(8,128)(2,1)} %param.25), channel_id=1, source_target_pairs={{0,16},{16,0},{1,17},{17,1},{2,18},{18,2},{3,19},{19,3},{4,20},{20... | collective-permute-start | bytes 4718600 | tf_op jit(solution)/shard_map/ppermute | solution.py:42
  81.3 16.0 %collective-permute-start.3 = (bf16[2,64,1024]{2,1,0:T(8,128)(2,1)}, bf16[2,64,1024]{2,1,0:T(8,128)(2,1)S(1)}, u32[]{:S(2)}, u32[]{:S(2)}) collective-permute-start(bf16[2,64,1024]{2,1,0:T(8,128)(2,1)} %reduce-scatter.7.cloned.1.call-done), channel_id=1, source_target_pairs={{0,16},{16,0},{1,17},{17,1},{2,18},{18,2},{3,19},{19,3},{4,20},{20... | collective-permute-start | bytes 786440 | tf_op jit(solution)/shard_map/ppermute | solution.py:125
  100.3 63.3 %all-gather.5.cloned.1.call-start = ((), (), s32[]{:S(2)}) async-start(), calls=%async_computation.12 | async-start | bytes 1392640 | tf_op jit(solution)/shard_map/all_gather | solution.py:163
  104.1 69.6 %collective-permute-start.5 = (bf16[1,2048,768]{2,1,0:T(8,128)(2,1)}, bf16[1,2048,768]{2,1,0:T(8,128)(2,1)}, u32[]{:S(2)}, u32[]{:S(2)}) collective-permute-start(bf16[1,2048,768]{2,1,0:T(8,128)(2,1)} %pad_maximum_fusion), channel_id=1, source_target_pairs={{0,16},{16,0},{1,17},{17,1},{2,18},{18,2},{3,19},{19,3},{4,20},{20... | collective-permute-start | bytes 9437192 | tf_op jit(solution)/shard_map/ppermute | solution.py:42
  134.9 4.9 %copy-start.6 = (bf16[256,2176]{1,0:T(8,128)(2,1)S(1)}, bf16[256,2176]{1,0:T(8,128)(2,1)}, u32[]{:S(2)}) copy-start(bf16[256,2176]{1,0:T(8,128)(2,1)} %all-gather.3.cloned.1.call-done) | copy-start | bytes 3342340
  134.9 4.9 %copy-start.14 = (bf16[2048,16]{0,1:T(8,128)(2,1)S(1)}, bf16[2048,16]{0,1:T(8,128)(2,1)}, u32[]{:S(2)}) copy-start(bf16[2048,16]{0,1:T(8,128)(2,1)} %param.23) | copy-start | bytes 196612
  135.0 34.1 %all-to-all-start = ((bf16[4,144,2048]{2,1,0:T(8,128)(2,1)}), bf16[4,144,2048]{2,1,0:T(8,128)(2,1)}, u32[]{:S(2)}, u32[]{:S(2)}) async-start(bf16[4,144,2048]{2,1,0:T(8,128)(2,1)} %bitcast.119), calls=%async_computation.2 | async-start | bytes 4718592 | tf_op jit(solution)/shard_map/all_to_all | solution.py:193
  169.0 4.7 %copy-start.13 = (bf16[1,2048,384]{2,1,0:T(8,128)(2,1)S(1)}, bf16[1,2048,384]{2,1,0:T(8,128)(2,1)}, u32[]{:S(2)}) copy-start(bf16[1,2048,384]{2,1,0:T(8,128)(2,1)} %param.25) | copy-start | bytes 4718596
  169.0 33.2 %all-to-all-start.2 = ((bf16[4,144,2048]{2,1,0:T(8,128)(2,1)}), bf16[4,144,2048]{2,1,0:T(8,128)(2,1)}, u32[]{:S(2)}, u32[]{:S(2)}) async-start(bf16[4,144,2048]{2,1,0:T(8,128)(2,1)} %bitcast.120), calls=%async_computation.5 | async-start | bytes 4718592 | tf_op jit(solution)/shard_map/all_to_all | solution.py:193
  202.2 33.1 %all-to-all-start.1 = ((bf16[4,144,2048]{2,1,0:T(8,128)(2,1)}), bf16[4,144,2048]{2,1,0:T(8,128)(2,1)}, u32[]{:S(2)}, u32[]{:S(2)}) async-start(bf16[4,144,2048]{2,1,0:T(8,128)(2,1)} %bitcast.128), calls=%async_computation.3 | async-start | bytes 4718592 | tf_op jit(solution)/shard_map/all_to_all | solution.py:202
  235.3 33.1 %all-to-all-start.3 = ((bf16[4,144,2048]{2,1,0:T(8,128)(2,1)}), bf16[4,144,2048]{2,1,0:T(8,128)(2,1)}, u32[]{:S(2)}, u32[]{:S(2)}) async-start(bf16[4,144,2048]{2,1,0:T(8,128)(2,1)} %bitcast.127), calls=%async_computation.6 | async-start | bytes 4718592 | tf_op jit(solution)/shard_map/all_to_all | solution.py:202
  239.8 35.5 %reduce-scatter.9.cloned.1.call-start = ((), (), s32[]{:S(2)}) async-start(), calls=%async_computation.11 | async-start | bytes 1310720 | tf_op jit(solution)/shard_map/reduce_scatter | solution.py:211
  246.6 55.3 %reduce-scatter.11.cloned.1.call-start = ((), (), s32[]{:S(2)}) async-start(), calls=%async_computation.13 | async-start | bytes 1310720 | tf_op jit(solution)/shard_map/reduce_scatter | solution.py:211
  248.9 19.5 %copy-start.4 = (f32[576,256]{1,0:T(8,128)}, f32[576,256]{1,0:T(8,128)S(1)}, u32[]{:S(2)}) copy-start(f32[576,256]{1,0:T(8,128)S(1)} %select_reduce_fusion) | copy-start | bytes 1769476
  271.1 32.7 %copy-start.1 = (bf16[1024,1024]{1,0:T(8,128)(2,1)S(1)}, bf16[1024,1024]{1,0:T(8,128)(2,1)}, u32[]{:S(2)}) copy-start(bf16[1024,1024]{1,0:T(8,128)(2,1)} %param.20) | copy-start | bytes 6291460
  (7 other events, 16.9 us)
Sparse Core Ops, SparseCore 0:
  27.7 25.2 reduce-scatter.4
  55.8 25.5 reduce-scatter.6
  100.4 29.0 all-gather.2
  135.1 28.4 all-gather.4
  246.7 27.0 reduce-scatter.8
  276.0 25.7 reduce-scatter.10
where the time goes:
time: 312 us; the launch traced here: 311 us
  waiting for transfers between devices  177 us (57%)
  matrix products  60.9 us (20%)
  starting transfers between devices  26.6 us (9%)
  other arithmetic  17.6 us (6%)
  local copies, waits for them, and re-layouts  14.3 us (5%)
  between operations  14 us (4%)
    all_gather x2, waiting for transfers between devices, shards(): rows_all = lax.all_gather(rows, 'ep', axis=0, tiled=True)  47.2 us
    all_to_all x2, waiting for transfers between devices, shards(): lax.all_to_all(served, 'tp', split_axis=0, concat_axis=0, tiled=True)  31.1 us
    reduce_scatter x2, waiting for transfers between devices, shards(): lax.psum_scatter(partial.astype(jnp.bfloat16).reshape(n_ep, share, width)...  26.5 us
    ppermute x5, waiting for transfers between devices, cp_pieces(): pieces.append(lax.ppermute(x, 'cp', perm))  24.9 us
    reduce_scatter x2, waiting for transfers between devices, shards(): lax.psum_scatter(block.astype(jnp.bfloat16), 'tp', scatter_dimension=1, t...  24.5 us
    dot_general x2, matrix products, expert_rows(): jnp.einsum('rf,df->rd', hidden_act, full_down[0], preferred_element_type=...  18.8 us
    ppermute x1, waiting for transfers between devices, shards(): lax.ppermute(summed, 'cp', [(i, (i - j) % n_cp) for i in range(n_cp)])  14.3 us
    dot_general x2, matrix products, expert_rows(): jnp.dot(flat_rows, full_gate[0], preferred_element_type=jnp.float32)  11.2 us
  transfers between devices with their start and end apart: 16, of which 10 were waited for; matrix products, arithmetic and copies ran while one was open for 25% of the time, Pallas kernels for 0%

commit v1 on v0

--- a/solution.py
+++ b/solution.py
@@ -5,6 +5,28 @@
 from jax.sharding import PartitionSpec as P
 
 HEAD_WIDTH = 128
+
+
+def joined_along(parts, dim):
+    parts = jnp.moveaxis(parts, 0, dim)
+    shape = parts.shape
+    return parts.reshape(*shape[:dim], shape[dim] * shape[dim + 1], *shape[dim + 2 :])
+
+
+def collect(x, axis, dim):
+    size = lax.axis_size(axis)
+    pairs = [(i, (i + 1) % size) for i in range(size)]
+    back = [(b, a) for a, b in pairs]
+    lower, upper = ([], [])
+    for hop in range(size - 1):
+        if hop % 2 == 0:
+            lower.append(lax.ppermute(lower[-1] if lower else x, axis, pairs))
+        else:
+            upper.append(lax.ppermute(upper[-1] if upper else x, axis, back))
+    parts = jnp.stack([*lower[::-1], x, *upper])
+    shift = lax.axis_index(axis) - len(lower)
+    parts = parts[(jnp.arange(size) - shift) % size]
+    return joined_along(parts, dim)
 
 
 def root_mean_scale(entries, gain):
@@ -160,7 +182,7 @@
         rows = rows_with_ids[chunk * share : (chunk + 1) * share]
         if chunk > 0:
             rows, _ = lax.optimization_barrier((rows, buffer))
-        rows_all = lax.all_gather(rows, "ep", axis=0, tiled=True)
+        rows_all = collect(rows, "ep", 0)
         normed_all = rows_all[:, :width]
         ids_all = rows_all[:, width : width + top_count].astype(jnp.int32)
         logits = jnp.dot(normed_all, router_weight, preferred_element_type=jnp.float32)

time: 312 us -> 358 us (1.15)
  waiting for transfers between devices: 177 us -> 210 us
  starting transfers between devices: 26.6 us -> 36.5 us
    all_gather x2 -> x0, waiting for transfers between devices: 47.2 us -> none  [shards(): rows_all = lax.all_gather(rows, 'ep', axis=0, tiled=True)]
    all_to_all x2, waiting for transfers between devices: 8.64 us -> 45.3 us  [shards(): lax.all_to_all(buffer.reshape(n_tp, cap2, width), 'tp', split_axis=0, con...]
    ppermute x0 -> x6, waiting for transfers between devices: none -> 31.4 us  [the longest x4 26.4 us: collect(): lower.append(lax.ppermute(lower[-1] if lower else x, axis, pairs))]
    ppermute x5, waiting for transfers between devices: 24.9 us -> 37.8 us  [cp_pieces(): pieces.append(lax.ppermute(x, 'cp', perm))]
    ppermute x0 -> x6, starting transfers between devices: none -> 9.38 us  [the longest x2 6.15 us: collect(): upper.append(lax.ppermute(upper[-1] if upper else x, axis, back))]
    gather x0 -> x2, local copies, waits for them, and re-layouts: none -> 4.86 us  [collect(): parts = parts[(jnp.arange(size) - shift) % size]]
  transfers between devices with their start and end apart: 16 -> 20, of which waited for: 10 -> 16; matrix products, arithmetic and copies ran while one was open for 25% -> 15% of each run, Pallas kernels for 0% -> 0%
where the time goes in v1:
time: 358 us; the launch traced here: 357 us
  waiting for transfers between devices  210 us (59%)
  matrix products  60.2 us (17%)
  starting transfers between devices  36.5 us (10%)
  other arithmetic  19.5 us (5%)
  local copies, waits for them, and re-layouts  17.4 us (5%)
  between operations  13.7 us (4%)
    all_to_all x2, waiting for transfers between devices, shards(): lax.all_to_all(buffer.reshape(n_tp, cap2, width), 'tp', split_axis=0, con...  45.3 us
    ppermute x5, waiting for transfers between devices, cp_pieces(): pieces.append(lax.ppermute(x, 'cp', perm))  37.8 us
    all_to_all x2, waiting for transfers between devices, shards(): lax.all_to_all(served, 'tp', split_axis=0, concat_axis=0, tiled=True)  31.2 us
    ppermute x4, waiting for transfers between devices, collect(): lower.append(lax.ppermute(lower[-1] if lower else x, axis, pairs))  26.4 us
    reduce_scatter x2, waiting for transfers between devices, shards(): lax.psum_scatter(partial.astype(jnp.bfloat16).reshape(n_ep, share, width)...  25.4 us
    reduce_scatter x2, waiting for transfers between devices, shards(): lax.psum_scatter(block.astype(jnp.bfloat16), 'tp', scatter_dimension=1, t...  24.5 us
    dot_general x2, matrix products, expert_rows(): jnp.einsum('rf,df->rd', hidden_act, full_down[0], preferred_element_type=...  18.8 us
    ppermute x1, waiting for transfers between devices, shards(): lax.ppermute(summed, 'cp', [(i, (i - j) % n_cp) for i in range(n_cp)])  14.3 us
  transfers between devices with their start and end apart: 20, of which 16 were waited for; matrix products, arithmetic and copies ran while one was open for 15% of the time, Pallas kernels for 0%

profile of v1, /device:TPU:0, one launch (start us, length us, event | category | flops | bytes accessed | tf_op | source)
XLA Modules:
  0.0 357.2 jit_solution(12870868675964018986)
XLA Ops:
  30.2 23.3 %collective-permute-done.2 = bf16[512,1024]{1,0:T(8,128)(2,1)S(1)} collective-permute-done((bf16[512,1024]{1,0:T(8,128)(2,1)S(1)}, bf16[512,1024]{1,0:T(8,128)(2,1)S(1)}, u32[]{:S(2)}, u32[]{:S(2)}) %collective-permute-start.2) | collective-permute-done | bytes 1048608 | tf_op jit(solution)/shard_map/ppermute | solution.py:64
  56.9 24.5 %reduce-scatter.7.cloned.1.call-done = bf16[2,64,1024]{2,1,0:T(8,128)(2,1)} async-done(((bf16[2,256,1024]{2,1,0:T(8,128)(2,1)}), bf16[2,64,1024]{2,1,0:T(8,128)(2,1)}) %reduce-scatter.7.cloned.1.call-update) | async-done | bytes 262160 | tf_op jit(solution)/shard_map/reduce_scatter | solution.py:145
  83.0 14.3 %collective-permute-done.3 = bf16[2,64,1024]{2,1,0:T(8,128)(2,1)S(1)} collective-permute-done((bf16[2,64,1024]{2,1,0:T(8,128)(2,1)}, bf16[2,64,1024]{2,1,0:T(8,128)(2,1)S(1)}, u32[]{:S(2)}, u32[]{:S(2)}) %collective-permute-start.3) | collective-permute-done | bytes 262176 | tf_op jit(solution)/shard_map/ppermute | solution.py:147
  103.4 7.6 %collective-permute-done.5 = bf16[64,2176]{1,0:T(8,128)(2,1)S(1)} collective-permute-done((bf16[64,2176]{1,0:T(8,128)(2,1)S(1)}, bf16[64,2176]{1,0:T(8,128)(2,1)S(1)}, u32[]{:S(2)}, u32[]{:S(2)}) %collective-permute-start.5) | collective-permute-done | bytes 278560 | tf_op jit(solution)/shard_map/ppermute | solution.py:23
  115.5 4.9 %collective-permute-done.6 = bf16[64,2176]{1,0:T(8,128)(2,1)S(1)} collective-permute-done((bf16[64,2176]{1,0:T(8,128)(2,1)S(1)}, bf16[64,2176]{1,0:T(8,128)(2,1)S(1)}, u32[]{:S(2)}, u32[]{:S(2)}) %collective-permute-start.6) | collective-permute-done | bytes 278560 | tf_op jit(solution)/shard_map/ppermute | solution.py:23
  126.9 3.8 %collective-permute-start.11 = (bf16[64,2176]{1,0:T(8,128)(2,1)S(1)}, bf16[64,2176]{1,0:T(8,128)(2,1)S(1)}, u32[]{:S(2)}, u32[]{:S(2)}) collective-permute-start(bf16[64,2176]{1,0:T(8,128)(2,1)S(1)} %get-tuple-element.34), channel_id=1, source_target_pairs={{1,0},{2,1},{3,2},{0,3},{5,4},{6,5},{7,6},{4,7},{9,8},{10,9},{11,1... | collective-permute-start | bytes 835592 | tf_op jit(solution)/shard_map/ppermute | solution.py:25
  130.7 7.7 %collective-permute-done.9 = bf16[64,2176]{1,0:T(8,128)(2,1)S(1)} collective-permute-done((bf16[64,2176]{1,0:T(8,128)(2,1)S(1)}, bf16[64,2176]{1,0:T(8,128)(2,1)S(1)}, u32[]{:S(2)}, u32[]{:S(2)}) %collective-permute-start.9) | collective-permute-done | bytes 278560 | tf_op jit(solution)/shard_map/ppermute | solution.py:23
  140.6 6.3 %collective-permute-done.10 = bf16[64,2176]{1,0:T(8,128)(2,1)S(1)} collective-permute-done((bf16[64,2176]{1,0:T(8,128)(2,1)S(1)}, bf16[64,2176]{1,0:T(8,128)(2,1)S(1)}, u32[]{:S(2)}, u32[]{:S(2)}) %collective-permute-start.10) | collective-permute-done | bytes 278560 | tf_op jit(solution)/shard_map/ppermute | solution.py:23
  156.4 4.7 %all-to-all-start.2 = ((bf16[4,144,2048]{2,1,0:T(8,128)(2,1)}), bf16[4,144,2048]{2,1,0:T(8,128)(2,1)}, u32[]{:S(2)}, u32[]{:S(2)}) async-start(bf16[4,144,2048]{2,1,0:T(8,128)(2,1)} %bitcast.133), calls=%async_computation.5 | async-start | bytes 4718592 | tf_op jit(solution)/shard_map/all_to_all | solution.py:215
  166.7 23.0 %all-to-all-done.2 = bf16[4,144,2048]{2,1,0:T(8,128)(2,1)} async-done(((bf16[4,144,2048]{2,1,0:T(8,128)(2,1)}), bf16[4,144,2048]{2,1,0:T(8,128)(2,1)}, u32[]{:S(2)}, u32[]{:S(2)}) %all-to-all-start.2) | async-done | bytes 2359328 | tf_op jit(solution)/shard_map/all_to_all | solution.py:215
  189.7 4.6 %all-to-all-start = ((bf16[4,144,2048]{2,1,0:T(8,128)(2,1)}), bf16[4,144,2048]{2,1,0:T(8,128)(2,1)}, u32[]{:S(2)}, u32[]{:S(2)}) async-start(bf16[4,144,2048]{2,1,0:T(8,128)(2,1)} %bitcast.132), calls=%async_computation.2 | async-start | bytes 4718592 | tf_op jit(solution)/shard_map/all_to_all | solution.py:215
  194.8 5.8 %fusion.19 = f32[576,768]{1,0:T(8,128)} fusion(bf16[576,2048]{1,0:T(8,128)(2,1)} %bitcast.37, bf16[1,2048,384]{2,1,0:T(8,128)(2,1)} %collective-permute-done.4, bf16[1,2048,384]{2,1,0:T(8,128)(2,1)} %param.25), kind=kOutput, calls=%fused_computation.39 | convolution fusion | flops 1818230784 | bytes 7274496 | tf_op jit(solution)/shard_map/dot_general | solution.py:71
  200.5 22.3 %all-to-all-done = bf16[4,144,2048]{2,1,0:T(8,128)(2,1)} async-done(((bf16[4,144,2048]{2,1,0:T(8,128)(2,1)}), bf16[4,144,2048]{2,1,0:T(8,128)(2,1)}, u32[]{:S(2)}, u32[]{:S(2)}) %all-to-all-start) | async-done | bytes 2359328 | tf_op jit(solution)/shard_map/all_to_all | solution.py:215
  222.9 12.9 %collective-permute-done.8 = bf16[1,2048,768]{2,1,0:T(8,128)(2,1)} collective-permute-done((bf16[1,2048,768]{2,1,0:T(8,128)(2,1)}, bf16[1,2048,768]{2,1,0:T(8,128)(2,1)}, u32[]{:S(2)}, u32[]{:S(2)}) %collective-permute-start.8) | collective-permute-done | bytes 3145760 | tf_op jit(solution)/shard_map/ppermute | solution.py:64
  235.7 5.1 %fusion.84 = (bf16[1,2048,384]{2,1,0:T(8,128)(2,1)S(1)}, bf16[1,2048,384]{2,1,0:T(8,128)(2,1)}, bf16[1,2048,384]{2,1,0:T(8,128)(2,1)}, bf16[1,2048,384]{2,1,0:T(8,128)(2,1)}) fusion(bf16[1,2048,768]{2,1,0:T(8,128)(2,1)} %pad_maximum_fusion, bf16[1,2048,768]{2,1,0:T(8,128)(2,1)} %collective-permute-done.8), kind=kLoop, calls=%fused_computation.169 | loop fusion | bytes 12582912 | tf_op jit(solution)/shard_map/slice | solution.py:221
  240.8 9.4 %convolution_convert_fusion = bf16[576,2048]{1,0:T(8,128)(2,1)} fusion(bf16[1,2048,384]{2,1,0:T(8,128)(2,1)} %get-tuple-element.58, bf16[1,2048,384]{2,1,0:T(8,128)(2,1)} %get-tuple-element.50, f32[576,768]{1,0:T(8,128)} %fusion.19, bf16[576,2048]{1,0:T(8,128)(2,1)} %bitcast.37, bf16[1,2048,384]{2,1,0:T(8,128)(2,1)} %get-tuple-element.59, ...), kind=kOutput, calls=%fused_computation.19 | convolution fusion | flops 3640295424 | bytes 12779520 | tf_op jit(solution)/shard_map/rf,df->rd/dot_general | solution.py:74
  250.3 4.7 %all-to-all-start.3 = ((bf16[4,144,2048]{2,1,0:T(8,128)(2,1)}), bf16[4,144,2048]{2,1,0:T(8,128)(2,1)}, u32[]{:S(2)}, u32[]{:S(2)}) async-start(bf16[4,144,2048]{2,1,0:T(8,128)(2,1)} %bitcast.147), calls=%async_computation.6 | async-start | bytes 4718592 | tf_op jit(solution)/shard_map/all_to_all | solution.py:224
  256.4 5.8 %fusion.20 = f32[576,768]{1,0:T(8,128)} fusion(bf16[576,2048]{1,0:T(8,128)(2,1)} %bitcast.22, bf16[1,2048,384]{2,1,0:T(8,128)(2,1)} %collective-permute-done.4, bf16[1,2048,384]{2,1,0:T(8,128)(2,1)} %param.25), kind=kOutput, calls=%fused_computation.40 | convolution fusion | flops 1818230784 | bytes 7274496 | tf_op jit(solution)/shard_map/dot_general | solution.py:71
  262.3 9.4 %convolution_convert_fusion.1 = bf16[576,2048]{1,0:T(8,128)(2,1)} fusion(bf16[1,2048,384]{2,1,0:T(8,128)(2,1)} %get-tuple-element.58, bf16[1,2048,384]{2,1,0:T(8,128)(2,1)} %get-tuple-element.50, f32[576,768]{1,0:T(8,128)} %fusion.20, bf16[576,2048]{1,0:T(8,128)(2,1)} %bitcast.22, bf16[1,2048,384]{2,1,0:T(8,128)(2,1)} %get-tuple-element.59, ...), kind=kOutput, calls=%fused_computation.20 | convolution fusion | flops 3640295424 | bytes 12779520 | tf_op jit(solution)/shard_map/rf,df->rd/dot_general | solution.py:74
  271.7 11.7 %all-to-all-done.3 = bf16[4,144,2048]{2,1,0:T(8,128)(2,1)} async-done(((bf16[4,144,2048]{2,1,0:T(8,128)(2,1)}), bf16[4,144,2048]{2,1,0:T(8,128)(2,1)}, u32[]{:S(2)}, u32[]{:S(2)}) %all-to-all-start.3) | async-done | bytes 2359328 | tf_op jit(solution)/shard_map/all_to_all | solution.py:224
  283.3 4.5 %all-to-all-start.1 = ((bf16[4,144,2048]{2,1,0:T(8,128)(2,1)}), bf16[4,144,2048]{2,1,0:T(8,128)(2,1)}, u32[]{:S(2)}, u32[]{:S(2)}) async-start(bf16[4,144,2048]{2,1,0:T(8,128)(2,1)} %bitcast.146), calls=%async_computation.3 | async-start | bytes 4718592 | tf_op jit(solution)/shard_map/all_to_all | solution.py:224
  296.9 19.5 %all-to-all-done.1 = bf16[4,144,2048]{2,1,0:T(8,128)(2,1)} async-done(((bf16[4,144,2048]{2,1,0:T(8,128)(2,1)}), bf16[4,144,2048]{2,1,0:T(8,128)(2,1)}, u32[]{:S(2)}, u32[]{:S(2)}) %all-to-all-start.1) | async-done | bytes 2359328 | tf_op jit(solution)/shard_map/all_to_all | solution.py:224
  319.1 4.2 %fusion.9 = bf16[256,2048]{1,0:T(8,128)(2,1)} fusion(f32[256,2048]{1,0:T(8,128)S(1)} %fusion.45, bf16[576,2048]{1,0:T(8,128)(2,1)} %bitcast.27, f32[576,256]{1,0:T(8,128)} %copy-done.4), kind=kOutput, calls=%fused_computation.25 | convolution fusion | flops 605618176 | bytes 6094848 | tf_op jit(solution)/shard_map/dot_general | solution.py:231
  323.3 25.4 %reduce-scatter.9.cloned.1.call-done = bf16[1,64,2048]{2,1,0:T(8,128)(2,1)} async-done(((bf16[4,64,2048]{2,1,0:T(8,128)(2,1)}), bf16[1,64,2048]{2,1,0:T(8,128)(2,1)}) %reduce-scatter.9.cloned.1.call-update) | async-done | bytes 262160 | tf_op jit(solution)/shard_map/reduce_scatter | solution.py:233
  (136 shorter events, 78.4 us)
Async XLA Ops:
  6.5 46.9 %reduce-scatter.5.cloned.1.call-start = ((), (), s32[]{:S(2)}) async-start(), calls=%async_computation.8 | async-start | bytes 1310720 | tf_op jit(solution)/shard_map/reduce_scatter | solution.py:145
  6.5 11.9 %collective-permute-start.1 = (s32[2,256]{1,0:T(2,128)}, s32[2,256]{1,0:T(2,128)S(1)}, u32[]{:S(2)}, u32[]{:S(2)}) collective-permute-start(s32[2,256]{1,0:T(2,128)} %param.17), channel_id=1, source_target_pairs={{0,16},{16,0},{1,17},{17,1},{2,18},{18,2},{3,19},{19,3},{4,20},{20... | collective-permute-start | bytes 6152 | tf_op jit(solution)/shard_map/ppermute | solution.py:64
  12.6 7.8 %collective-permute-start = (bf16[2,256,256]{2,1,0:T(8,128)(2,1)S(1)}, bf16[2,256,256]{2,1,0:T(8,128)(2,1)S(1)}, u32[]{:S(2)}, u32[]{:S(2)}) collective-permute-start(bf16[2,256,256]{2,1,0:T(8,128)(2,1)S(1)} %pad_maximum_fusion.4), channel_id=1, source_target_pairs={{0,16},{16,0},{1,17},{17,1},{2,18},{18,2},{3,19},{19,3},{4,20},{20... | collective-permute-start | bytes 786440 | tf_op jit(solution)/shard_map/ppermute | solution.py:64
  27.6 53.8 %reduce-scatter.7.cloned.1.call-start = ((), (), s32[]{:S(2)}) async-start(), calls=%async_computation.9 | async-start | bytes 1310720 | tf_op jit(solution)/shard_map/reduce_scatter | solution.py:145
  29.6 27.2 %copy-start.13 = (s32[2,256,8]{1,2,0:T(8,128)S(1)}, s32[2,256,8]{1,2,0:T(8,128)}, u32[]{:S(2)}) copy-start(s32[2,256,8]{1,2,0:T(8,128)} %param.24) | copy-start | bytes 49156
  29.7 23.8 %collective-permute-start.2 = (bf16[512,1024]{1,0:T(8,128)(2,1)S(1)}, bf16[512,1024]{1,0:T(8,128)(2,1)S(1)}, u32[]{:S(2)}, u32[]{:S(2)}) collective-permute-start(bf16[512,1024]{1,0:T(8,128)(2,1)S(1)} %bitcast.151), channel_id=1, source_target_pairs={{0,16},{16,0},{1,17},{17,1},{2,18},{18,2},{3,19},{19,3},{4,20},{20... | collective-permute-start | bytes 3145736 | tf_op jit(solution)/shard_map/ppermute | solution.py:64
  53.4 43.9 %copy-start.10 = (bf16[2,64,1024]{2,1,0:T(8,128)(2,1)S(1)}, bf16[2,64,1024]{2,1,0:T(8,128)(2,1)}, u32[]{:S(2)}) copy-start(bf16[2,64,1024]{2,1,0:T(8,128)(2,1)} %reduce-scatter.5.cloned.1.call-done) | copy-start | bytes 786436
  55.7 43.6 %collective-permute-start.4 = (bf16[1,2048,384]{2,1,0:T(8,128)(2,1)}, bf16[1,2048,384]{2,1,0:T(8,128)(2,1)}, u32[]{:S(2)}, u32[]{:S(2)}) collective-permute-start(bf16[1,2048,384]{2,1,0:T(8,128)(2,1)} %param.25), channel_id=1, source_target_pairs={{0,16},{16,0},{1,17},{17,1},{2,18},{18,2},{3,19},{19,3},{4,20},{20... | collective-permute-start | bytes 4718600 | tf_op jit(solution)/shard_map/ppermute | solution.py:64
  81.4 15.9 %collective-permute-start.3 = (bf16[2,64,1024]{2,1,0:T(8,128)(2,1)}, bf16[2,64,1024]{2,1,0:T(8,128)(2,1)S(1)}, u32[]{:S(2)}, u32[]{:S(2)}) collective-permute-start(bf16[2,64,1024]{2,1,0:T(8,128)(2,1)} %reduce-scatter.7.cloned.1.call-done), channel_id=1, source_target_pairs={{0,16},{16,0},{1,17},{17,1},{2,18},{18,2},{3,19},{19,3},{4,20},{20... | collective-permute-start | bytes 786440 | tf_op jit(solution)/shard_map/ppermute | solution.py:147
  99.5 11.4 %collective-permute-start.5 = (bf16[64,2176]{1,0:T(8,128)(2,1)S(1)}, bf16[64,2176]{1,0:T(8,128)(2,1)S(1)}, u32[]{:S(2)}, u32[]{:S(2)}) collective-permute-start(bf16[64,2176]{1,0:T(8,128)(2,1)S(1)} %get-tuple-element.55), channel_id=1, source_target_pairs={{0,1},{1,2},{2,3},{3,0},{4,5},{5,6},{6,7},{7,4},{8,9},{9,10},{10,1... | collective-permute-start | bytes 835592 | tf_op jit(solution)/shard_map/ppermute | solution.py:23
  101.0 14.4 %collective-permute-start.7 = (bf16[64,2176]{1,0:T(8,128)(2,1)S(1)}, bf16[64,2176]{1,0:T(8,128)(2,1)S(1)}, u32[]{:S(2)}, u32[]{:S(2)}) collective-permute-start(bf16[64,2176]{1,0:T(8,128)(2,1)S(1)} %get-tuple-element.55), channel_id=1, source_target_pairs={{1,0},{2,1},{3,2},{0,3},{5,4},{6,5},{7,6},{4,7},{9,8},{10,9},{11,1... | collective-permute-start | bytes 835592 | tf_op jit(solution)/shard_map/ppermute | solution.py:25
  110.9 9.4 %collective-permute-start.6 = (bf16[64,2176]{1,0:T(8,128)(2,1)S(1)}, bf16[64,2176]{1,0:T(8,128)(2,1)S(1)}, u32[]{:S(2)}, u32[]{:S(2)}) collective-permute-start(bf16[64,2176]{1,0:T(8,128)(2,1)S(1)} %collective-permute-done.5), channel_id=1, source_target_pairs={{0,1},{1,2},{2,3},{3,0},{4,5},{5,6},{6,7},{7,4},{8,9},{9,10},{10,1... | collective-permute-start | bytes 835592 | tf_op jit(solution)/shard_map/ppermute | solution.py:23
  123.4 24.6 %copy-start.5 = (bf16[4,64,2176]{2,1,0:T(8,128)(2,1)}, bf16[4,64,2176]{2,1,0:T(8,128)(2,1)S(1)}, u32[]{:S(2)}) copy-start(bf16[4,64,2176]{2,1,0:T(8,128)(2,1)S(1)} %gather_fusion) | copy-start | bytes 3342340
  126.9 11.5 %collective-permute-start.9 = (bf16[64,2176]{1,0:T(8,128)(2,1)S(1)}, bf16[64,2176]{1,0:T(8,128)(2,1)S(1)}, u32[]{:S(2)}, u32[]{:S(2)}) collective-permute-start(bf16[64,2176]{1,0:T(8,128)(2,1)S(1)} %get-tuple-element.34), channel_id=1, source_target_pairs={{0,1},{1,2},{2,3},{3,0},{4,5},{5,6},{6,7},{7,4},{8,9},{9,10},{10,1... | collective-permute-start | bytes 835592 | tf_op jit(solution)/shard_map/ppermute | solution.py:23
  126.9 13.7 %collective-permute-start.11 = (bf16[64,2176]{1,0:T(8,128)(2,1)S(1)}, bf16[64,2176]{1,0:T(8,128)(2,1)S(1)}, u32[]{:S(2)}, u32[]{:S(2)}) collective-permute-start(bf16[64,2176]{1,0:T(8,128)(2,1)S(1)} %get-tuple-element.34), channel_id=1, source_target_pairs={{1,0},{2,1},{3,2},{0,3},{5,4},{6,5},{7,6},{4,7},{9,8},{10,9},{11,1... | collective-permute-start | bytes 835592 | tf_op jit(solution)/shard_map/ppermute | solution.py:25
  138.4 8.4 %collective-permute-start.10 = (bf16[64,2176]{1,0:T(8,128)(2,1)S(1)}, bf16[64,2176]{1,0:T(8,128)(2,1)S(1)}, u32[]{:S(2)}, u32[]{:S(2)}) collective-permute-start(bf16[64,2176]{1,0:T(8,128)(2,1)S(1)} %collective-permute-done.9), channel_id=1, source_target_pairs={{0,1},{1,2},{2,3},{3,0},{4,5},{5,6},{6,7},{7,4},{8,9},{9,10},{10,1... | collective-permute-start | bytes 835592 | tf_op jit(solution)/shard_map/ppermute | solution.py:23
  156.4 33.2 %all-to-all-start.2 = ((bf16[4,144,2048]{2,1,0:T(8,128)(2,1)}), bf16[4,144,2048]{2,1,0:T(8,128)(2,1)}, u32[]{:S(2)}, u32[]{:S(2)}) async-start(bf16[4,144,2048]{2,1,0:T(8,128)(2,1)} %bitcast.133), calls=%async_computation.5 | async-start | bytes 4718592 | tf_op jit(solution)/shard_map/all_to_all | solution.py:215
  164.4 71.3 %collective-permute-start.8 = (bf16[1,2048,768]{2,1,0:T(8,128)(2,1)}, bf16[1,2048,768]{2,1,0:T(8,128)(2,1)}, u32[]{:S(2)}, u32[]{:S(2)}) collective-permute-start(bf16[1,2048,768]{2,1,0:T(8,128)(2,1)} %pad_maximum_fusion), channel_id=1, source_target_pairs={{0,16},{16,0},{1,17},{17,1},{2,18},{18,2},{3,19},{19,3},{4,20},{20... | collective-permute-start | bytes 9437192 | tf_op jit(solution)/shard_map/ppermute | solution.py:64
  189.7 33.2 %all-to-all-start = ((bf16[4,144,2048]{2,1,0:T(8,128)(2,1)}), bf16[4,144,2048]{2,1,0:T(8,128)(2,1)}, u32[]{:S(2)}, u32[]{:S(2)}) async-start(bf16[4,144,2048]{2,1,0:T(8,128)(2,1)} %bitcast.132), calls=%async_computation.2 | async-start | bytes 4718592 | tf_op jit(solution)/shard_map/all_to_all | solution.py:215
  250.3 33.1 %all-to-all-start.3 = ((bf16[4,144,2048]{2,1,0:T(8,128)(2,1)}), bf16[4,144,2048]{2,1,0:T(8,128)(2,1)}, u32[]{:S(2)}, u32[]{:S(2)}) async-start(bf16[4,144,2048]{2,1,0:T(8,128)(2,1)} %bitcast.147), calls=%async_computation.6 | async-start | bytes 4718592 | tf_op jit(solution)/shard_map/all_to_all | solution.py:224
  283.3 33.1 %all-to-all-start.1 = ((bf16[4,144,2048]{2,1,0:T(8,128)(2,1)}), bf16[4,144,2048]{2,1,0:T(8,128)(2,1)}, u32[]{:S(2)}, u32[]{:S(2)}) async-start(bf16[4,144,2048]{2,1,0:T(8,128)(2,1)} %bitcast.146), calls=%async_computation.3 | async-start | bytes 4718592 | tf_op jit(solution)/shard_map/all_to_all | solution.py:224
  287.8 35.5 %reduce-scatter.11.cloned.1.call-start = ((), (), s32[]{:S(2)}) async-start(), calls=%async_computation.11 | async-start | bytes 1310720 | tf_op jit(solution)/shard_map/reduce_scatter | solution.py:233
  294.5 54.3 %reduce-scatter.9.cloned.1.call-start = ((), (), s32[]{:S(2)}) async-start(), calls=%async_computation.10 | async-start | bytes 1310720 | tf_op jit(solution)/shard_map/reduce_scatter | solution.py:233
  319.1 31.6 %copy-start.1 = (bf16[1024,1024]{1,0:T(8,128)(2,1)S(1)}, bf16[1024,1024]{1,0:T(8,128)(2,1)}, u32[]{:S(2)}) copy-start(bf16[1024,1024]{1,0:T(8,128)(2,1)} %param.20) | copy-start | bytes 6291460
  (12 other events, 67.7 us)
Sparse Core Ops, SparseCore 0:
  27.7 25.2 reduce-scatter.4
  55.8 25.4 reduce-scatter.6
  294.6 26.0 reduce-scatter.10
  323.4 25.2 reduce-scatter.8
